TPU v7x, 128 devices: a whole 4x4x4 slice. The times are simulated.
128 devices in a mesh: section: 2 (over core), seq: 64 (over z, x, y).
Axes of the slice: x: 4, y: 4, z: 4, core: 2. Of those that a mesh axis runs over, the one named last changes fastest.
Arguments:
- patches: bfloat16 [32768, 1408], P('seq'), may hold values from -42 to 42
- image_grid: int32 [256, 2], P('seq'), may hold values from 2 to 52, as said below
- image_offsets: int32 [256], P('seq'), may hold values from 0 to 32736, as said below
- dest_positions: int32 [8192], replicated, may hold values from 0 to 16383, as said below
- text_embeds: bfloat16 [256, 64, 1408], P(None, 'seq'), may hold values from -42 to 42
- segment_ids: int32 [256, 64], replicated, may hold values from 0 to 3, as said below
- vision_qkv: bfloat16 [1408, 3, 1408], P(None, None, 'section'), may hold values from -0.15625 to 0.15625
- vision_out: bfloat16 [1408, 1408], P('section'), may hold values from -0.875 to 0.875
- projector: bfloat16 [4, 1408, 1408], P('section'), may hold values from -0.078125 to 0.078125
- decoder_q: bfloat16 [1408, 1408], P(None, 'section'), may hold values from -0.15625 to 0.15625
- decoder_kv: bfloat16 [1408, 2, 176], P(None, None, 'section'), may hold values from -0.15625 to 0.15625
- decoder_out: bfloat16 [1408, 1408], P('section'), may hold values from -0.875 to 0.875
Outputs:
- decoded: bfloat16 [256, 64, 1408], P(None, 'seq')
Inputs may be any that keep to these rules, and one draw needn't show every extreme that they name: `image_grid`: patch rows and columns are even, columns are 8 or 16; the images of one index of seq lie back to back and cover exactly its 512 patches. `image_offsets`: each image's first patch; images are in order, back to back, the first of an index of seq at its first patch. `dest_positions`: the 128 merged rows of one index of seq go, in order, to 128 consecutive prompt positions; the ranges of different indices do not meet. `segment_ids`: never falls along prompt positions; every document number is used.
All inputs are finite; a program needn't handle non-finite values.
Results may differ from a plain program's by a relative error of at most 0.025.
Values may be sent and summed in bfloat16 or wider, within the bound.
No kernel may reach another device: no remote copies, remote signals or barrier semaphores. Data moves between devices by JAX's collectives and lax.ppermute only.
A program may use at most 128 MiB of HBM per device.

v0:
```python
import math

import jax
import jax.numpy as jnp
from jax import lax
from jax.sharding import PartitionSpec as P
from jax.experimental import pallas as pl
from jax.experimental.pallas import tpu as pltpu
import functools

D = 1408
HEAD = 88


def layer_norm(values):
    values = values.astype(jnp.float32)
    centred = values - jnp.mean(values, -1, keepdims=True)
    return centred * lax.rsqrt(jnp.mean(centred * centred, -1, keepdims=True) + 1e-06)


def root_norm(values):
    values = values.astype(jnp.float32)
    return values * lax.rsqrt(jnp.mean(values * values, -1, keepdims=True) + 1e-06)


def merge_rows(grid, offsets, count):
    heights = grid[:, 0]
    widths = grid[:, 1]
    group_start = offsets // 4
    group_count = heights * widths // 4
    merged_ids = jnp.arange(count, dtype=jnp.int32)
    inside = (
        (merged_ids[:, None] >= group_start[None, :])
        & (merged_ids[:, None] < (group_start + group_count)[None, :])
    ).astype(jnp.int32)
    first_group = jnp.sum(inside * group_start[None, :], 1)
    first_patch = jnp.sum(inside * offsets[None, :], 1)
    row_width = jnp.sum(inside * widths[None, :], 1)
    within = merged_ids - first_group
    groups_across = row_width // 2
    group_row = within // groups_across
    group_col = within % groups_across
    corner = first_patch + 2 * group_row * row_width + 2 * group_col
    return jnp.stack([corner, corner + 1, corner + row_width, corner + row_width + 1], 1)


def _segment_start(info_ref, places):
    start = jnp.zeros_like(places) + info_ref[0]
    for doc in range(1, 4):
        bound = info_ref[doc]
        start = jnp.where(places >= bound, bound, start)
    return start


def _first_block(info_ref, qb, span):
    return _segment_start(info_ref, qb * span + info_ref[4]) // span


def _text_kernel(query_block_ref, key_block_ref, info_ref, q_ref, kv_ref, o_ref, acc_ref, ext_ref, *, scale):
    step = pl.program_id(0)
    qb = query_block_ref[step]
    kb = key_block_ref[step]
    heads, rows, head = q_ref.shape
    shards = kv_ref.shape[0]
    span = rows * shards
    own = info_ref[4]
    last_query = qb * span + own + (rows - 1) * shards
    active = kb >= _first_block(info_ref, qb, span)
    unmasked = (kb < qb) & (kb * span >= _segment_start(info_ref, last_query))

    @pl.when(step == 0)
    def _():
        lane = lax.broadcasted_iota(jnp.int32, ext_ref.shape, 1)
        ext_ref[...] = jnp.where(lane == head, 1.0, 0.0).astype(ext_ref.dtype)

    @pl.when(kb == 0)
    def _():
        acc_ref[...] = jnp.zeros_like(acc_ref)

    def accumulate(masked):
        q = q_ref[...].reshape(heads * rows, head)
        k = kv_ref[:, 0].reshape(span, head)
        ext_ref[:, :head] = kv_ref[:, 1].reshape(span, head)
        s = lax.dot_general(q, k, (((1,), (1,)), ((), ())), preferred_element_type=jnp.float32)
        w = jnp.exp(s * scale)
        if masked:
            row = lax.broadcasted_iota(jnp.int32, (heads * rows, 1), 0) & (rows - 1)
            query_places = (qb * rows + row) * shards + own
            lane = lax.broadcasted_iota(jnp.int32, (1, span), 1)
            key_places = (kb * rows + (lane & (rows - 1))) * shards + lax.shift_right_logical(
                lane, rows.bit_length() - 1
            )
            allowed = (key_places <= query_places) & (
                key_places >= _segment_start(info_ref, query_places)
            )
            w = jnp.where(allowed, w, 0.0)
        acc_ref[...] += jnp.dot(
            w.astype(jnp.bfloat16), ext_ref[...], preferred_element_type=jnp.float32
        )

    @pl.when(active & unmasked)
    def _():
        accumulate(False)

    @pl.when(active & jnp.logical_not(unmasked))
    def _():
        accumulate(True)

    @pl.when(kb == qb)
    def _():
        acc = acc_ref[...]
        o_ref[...] = (acc[:, :head] / acc[:, head : head + 1]).astype(o_ref.dtype).reshape(
            o_ref.shape
        )


def text_attention(info, q, kv, rows, scale):
    heads, text_rows, head = q.shape
    shards = kv.shape[0]
    blocks = text_rows // rows
    span = rows * shards
    pairs = [(i, j) for i in range(blocks) for j in range(i + 1)]
    query_block = jnp.array([i for i, _ in pairs], jnp.int32)
    key_block = jnp.array([j for _, j in pairs], jnp.int32)

    def q_block(t, qb_ref, kb_ref, info_ref):
        return (0, qb_ref[t], 0)

    def kv_block(t, qb_ref, kb_ref, info_ref):
        qb = qb_ref[t]
        return (0, 0, jnp.maximum(kb_ref[t], _first_block(info_ref, qb, span)), 0)

    return pl.pallas_call(
        functools.partial(_text_kernel, scale=scale),
        grid_spec=pltpu.PrefetchScalarGridSpec(
            num_scalar_prefetch=3,
            grid=(len(pairs),),
            in_specs=[
                pl.BlockSpec((heads, rows, head), q_block),
                pl.BlockSpec((shards, 2, rows, head), kv_block),
            ],
            out_specs=pl.BlockSpec((heads, rows, head), q_block),
            scratch_shapes=[
                pltpu.VMEM((heads * rows, 128), jnp.float32),
                pltpu.VMEM((span, 128), jnp.bfloat16),
            ],
        ),
        out_shape=jax.ShapeDtypeStruct((heads, text_rows, head), jnp.bfloat16),
        compiler_params=pltpu.CompilerParams(dimension_semantics=("arbitrary",)),
    )(query_block, key_block, info, q, kv)


def swap(values):
    return lax.ppermute(values, "section", [(0, 1), (1, 0)])


def in_head_order(first, own, other, axis):
    return jnp.where(
        first, jnp.concatenate([own, other], axis), jnp.concatenate([other, own], axis)
    )


def body(
    patches,
    image_grid,
    image_offsets,
    dest_positions,
    text_embeds,
    segment_ids,
    vision_qkv,
    vision_out,
    projector,
    decoder_q,
    decoder_kv,
    decoder_out,
):
    section_index = lax.axis_index("section")
    seq_index = lax.axis_index("seq")
    seq_count = lax.axis_size("seq")
    first = section_index == 0
    scale = 3.0 / math.sqrt(HEAD)
    patch_count = patches.shape[0]
    local_heads = vision_out.shape[0] // HEAD
    merged_count = patch_count // 4

    vision_out_other = swap(vision_out)
    decoder_out_other = swap(decoder_out)

    normed = layer_norm(patches).astype(jnp.bfloat16)
    mixed = jnp.dot(normed, vision_qkv.reshape(D, -1), preferred_element_type=jnp.float32).reshape(
        patch_count, 3, local_heads, HEAD
    )
    queries = root_norm(mixed[:, 0]).astype(jnp.bfloat16)
    keys = root_norm(mixed[:, 1]).astype(jnp.bfloat16)
    values = mixed[:, 2].astype(jnp.bfloat16)
    offsets = image_offsets - seq_index * patch_count
    image_of = jnp.sum(
        (jnp.arange(patch_count, dtype=jnp.int32)[:, None] >= offsets[None, :]).astype(jnp.int32), 1
    )
    scores = jnp.einsum("qhd,khd->hqk", queries, keys, preferred_element_type=jnp.float32) * scale
    same = (image_of[:, None] == image_of[None, :])[None]
    weights = jnp.where(same, jnp.exp(scores), jnp.zeros_like(scores))
    totals = jnp.sum(weights, -1)
    mixed_values = jnp.einsum(
        "hqk,khd->qhd", weights.astype(jnp.bfloat16), values, preferred_element_type=jnp.float32
    )
    attended = (
        (mixed_values / jnp.transpose(totals)[:, :, None])
        .astype(jnp.bfloat16)
        .reshape(patch_count, local_heads * HEAD)
    )
    picks = merge_rows(image_grid, offsets, merged_count)
    own_picks = lax.dynamic_slice_in_dim(picks, 2 * section_index, 2, 1).reshape(-1)
    other_picks = lax.dynamic_slice_in_dim(picks, 2 - 2 * section_index, 2, 1).reshape(-1)
    patch_ids = jnp.arange(patch_count, dtype=jnp.int32)[None, :]
    own_select = (own_picks[:, None] == patch_ids).astype(jnp.bfloat16)
    other_select = (other_picks[:, None] == patch_ids).astype(jnp.bfloat16)
    received_heads = swap(
        jnp.dot(other_select, attended, preferred_element_type=jnp.float32).astype(jnp.bfloat16)
    )
    own_heads = jnp.dot(own_select, attended, preferred_element_type=jnp.float32).astype(
        jnp.bfloat16
    )
    own_rows = jnp.concatenate([own_heads, received_heads], 1)
    full_out = jnp.concatenate([vision_out, vision_out_other], 0)
    kept = (
        jnp.dot(own_select, patches, preferred_element_type=jnp.float32)
        + jnp.dot(own_rows, full_out, preferred_element_type=jnp.float32)
    ).astype(jnp.bfloat16)
    merge_terms = jnp.dot(
        kept.reshape(merged_count, 2 * D),
        projector.reshape(2 * D, D),
        preferred_element_type=jnp.float32,
    )
    image_rows = (merge_terms + swap(merge_terms)).astype(jnp.bfloat16)

    per_peer = merged_count // seq_count
    run_starts = dest_positions.reshape(seq_count, merged_count)[:, 0]
    own_start = run_starts[seq_index]
    received = lax.all_to_all(
        jnp.transpose(
            jnp.roll(image_rows.reshape(per_peer, seq_count, D), own_start, axis=1), (1, 0, 2)
        ),
        "seq",
        split_axis=0,
        concat_axis=0,
        tiled=True,
    )
    slot_base = jnp.arange(per_peer, dtype=jnp.int32)[:, None] * seq_count
    landing = (
        run_starts[None, :] + slot_base + (seq_index - run_starts[None, :]) % seq_count
    ) // seq_count
    text_rows = text_embeds.shape[0]
    prompt = text_embeds.reshape(text_rows, D).at[landing.T.reshape(-1)].set(received.reshape(-1, D))
    text_normed = root_norm(prompt).astype(jnp.bfloat16)
    head_queries = root_norm(
        jnp.einsum(
            "td,dhe->hte",
            text_normed,
            decoder_q.reshape(D, local_heads, HEAD),
            preferred_element_type=jnp.float32,
        )
    ).astype(jnp.bfloat16)
    paired = jnp.dot(
        text_normed, decoder_kv.reshape(D, -1), preferred_element_type=jnp.float32
    ).reshape(text_rows, 2, HEAD)
    key_rows = root_norm(paired[:, 0]).astype(jnp.bfloat16)
    value_rows = paired[:, 1].astype(jnp.bfloat16)

    shared = jnp.stack([key_rows, value_rows], 0)[None]
    piece = lax.all_gather(shared, "seq", axis=0, tiled=True)
    rows = 64
    doc_starts = jnp.sum(
        (segment_ids[None] < jnp.arange(4, dtype=jnp.int32)[:, None, None]).astype(jnp.int32),
        (1, 2),
    )
    info = jnp.concatenate(
        [doc_starts, jnp.full((1,), seq_index, jnp.int32), jnp.zeros((3,), jnp.int32)]
    )
    decoder_out_full, head_queries = lax.optimization_barrier(
        (in_head_order(first, decoder_out, decoder_out_other, 0), head_queries)
    )
    head_major = text_attention(info, head_queries, piece, rows, scale)
    attended_text = jnp.transpose(head_major, (1, 0, 2)).reshape(text_rows, -1)
    all_heads = in_head_order(first, attended_text, swap(attended_text), 1)
    output_terms = jnp.dot(all_heads, decoder_out_full, preferred_element_type=jnp.float32)
    decoded = (prompt.astype(jnp.float32) + output_terms).astype(jnp.bfloat16)
    return decoded.reshape(text_rows, 1, D)


def solution(mesh):
    placed = (
        P("seq", None),
        P("seq", None),
        P("seq"),
        P(),
        P(None, "seq", None),
        P(),
        P(None, None, "section"),
        P("section", None),
        P("section", None, None),
        P(None, "section"),
        P(None, None, "section"),
        P("section", None),
    )
    return jax.shard_map(
        body, mesh=mesh, in_specs=placed, out_specs=P(None, "seq", None), check_vma=False
    )
```

profile of v0, /device:TPU:1, one launch (start us, length us, event | category | flops | bytes accessed | tf_op | source)
XLA Modules:
  0.0 191.2 jit_solution(12793117811442989230)
XLA Ops:
  6.5 1.4 collective-permute-start.1
  8.0 0.7 slice_bitcast_fusion.2
  8.6 0.8 fusion.70
  9.6 0.1 broadcast_add_fusion.1
  9.9 0.1 eq.86
  10.0 1.6 convert_reduce_fusion
  11.7 0.5 fusion.13
  12.2 6.0 %fusion.29 = f32[512,3,8,88]{0,3,2,1:T(8,128)S(1)} fusion(bf16[3,8,88,1408]{3,2,1,0:T(8,128)(2,1)} %bitcast.130, bf16[512,1408]{1,0:T(8,128)(2,1)S(1)} %copy-done.2, f32[512]{0:T(512)S(1)} %add_rsqrt_fusion.3, f32[512]{0:T(512)S(1)} %broadcast_multiply_fusion), kind=kOutput, calls=%fused_computation.30 | convolution fusion | flops 3047948288 | bytes 11718656 | tf_op jit(solution)/shard_map/dot_general | solution.py:190
  18.2 0.4 multiply_reduce_fusion.1
  18.6 0.2 broadcast_compare_fusion
  18.9 2.5 %fusion = (f32[8,512]{1,0:T(8,128)S(1)}, f32[8,512,512]{1,2,0:T(8,128)S(1)}) fusion(pred[512,512]{0,1:T(8,128)(4,1)S(1)} %broadcast_compare_fusion, f32[512,3,8,88]{0,3,2,1:T(8,128)S(1)} %fusion.29, f32[512,8]{0,1:T(8,128)S(1)} %get-tuple-element.27, f32[512,8]{0,1:T(8,128)S(1)} %get-tuple-element.28), kind=kOutput, calls=%fused_computation.2 | convolution fusion | flops 376827904 | bytes 11583488 | tf_op jit(solution)/shard_map/qhd,khd->hqk/dot_general | solution.py:200
  21.4 1.8 divide_convert_fusion
  23.2 1.2 convolution_convert_fusion
  24.4 0.2 collective-permute-start
  24.7 0.1 eq.79
  24.8 1.7 convolution_convert_fusion.1
  26.6 0.6 fusion.53
  27.2 3.1 %fusion.19 = bf16[256,1408]{1,0:T(8,128)(2,1)S(1)} fusion(f32[256,1408]{1,0:T(8,128)S(1)} %fusion.53, bf16[704,1408]{1,0:T(8,128)(2,1)} %collective-permute-done.1, bf16[704,1408]{1,0:T(8,128)(2,1)S(1)} %copy-done.5, bf16[256,704]{0,1:T(8,128)(2,1)} %collective-permute-done, bf16[256,704]{0,1:T(8,128)(2,1)S(1)} %convolution_convert_fusion.1), kind=kOutput, calls=%fused_computation.22 | convolution fusion | flops 1025114112 | bytes 6848512 | tf_op jit(solution)/shard_map/dot_general | solution.py:228
  30.3 0.2 reshape.479
  30.6 4.5 %fusion.77 = f32[128,1408]{1,0:T(8,128)S(1)} fusion(bf16[128,2816]{1,0:T(8,128)(2,1)S(1)} %reshape.479, bf16[2816,1408]{1,0:T(8,128)(2,1)} %bitcast.122), kind=kOutput, calls=%fused_computation.150 | convolution fusion | flops 1015021568 | bytes 9371648 | tf_op jit(solution)/shard_map/dot_general | solution.py:230
  35.1 0.6 collective-permute-start.2
  35.8 0.5 constant_dynamic-slice_fusion
  38.3 1.2 add_convert_fusion
  39.5 0.4 copy.48
  39.9 1.7 fusion.56
  41.6 11.2 %all-to-all-start = ((bf16[64,2,1408]{2,1,0:T(2,128)(2,1)}), bf16[64,2,1408]{2,1,0:T(2,128)(2,1)S(1)}, u32[]{:S(2)}, u32[]{:S(2)}) async-start(bf16[64,2,1408]{2,1,0:T(2,128)(2,1)} %fusion.56), calls=%async_computation | async-start | bytes 720896 | tf_op jit(solution)/shard_map/all_to_all | solution.py:240
  52.9 0.1 add.316
  53.1 10.6 %all-to-all-done = bf16[64,2,1408]{2,1,0:T(2,128)(2,1)S(1)} async-done(((bf16[64,2,1408]{2,1,0:T(2,128)(2,1)}), bf16[64,2,1408]{2,1,0:T(2,128)(2,1)S(1)}, u32[]{:S(2)}, u32[]{:S(2)}) %all-to-all-start) | async-done | bytes 360480 | tf_op jit(solution)/shard_map/all_to_all | solution.py:240
  63.8 1.6 scatter_fusion
  65.4 0.2 fusion.26
  65.6 1.5 fusion.48
  67.2 0.7 pad_maximum_fusion
  67.9 1.8 collective-permute-start.3
  69.7 0.2 convert_reduce_fusion.1
  69.8 0.6 pad_add_fusion.1.info_ref
  70.4 3.2 %collective-permute-done.3 = bf16[704,1408]{1,0:T(8,128)(2,1)} collective-permute-done((bf16[704,1408]{1,0:T(8,128)(2,1)}, bf16[704,1408]{1,0:T(8,128)(2,1)}, u32[]{:S(2)}, u32[]{:S(2)}) %collective-permute-start.3) | collective-permute-done | bytes 1982496 | tf_op jit(solution)/shard_map/ppermute | solution.py:154
  73.6 6.2 %maximum_select_fusion = bf16[1408,1408]{1,0:T(8,128)(2,1)} fusion(bf16[704,1408]{1,0:T(8,128)(2,1)} %collective-permute-done.3, bf16[704,1408]{1,0:T(8,128)(2,1)} %param.25, pred[]{:T(512)S(6)} %eq.90), kind=kLoop, calls=%fused_computation.12 | loop fusion | flops 17842176 | bytes 7929857 | tf_op jit(solution)/shard_map/jit(_where)/select_n | solution.py:158
  79.9 0.8 fusion.58
  80.7 1.3 copy.50
  82.0 1.6 fusion.33
  83.6 2.4 %fusion.34.q_ref = bf16[8,256,88]{2,1,0:T(8,128)(2,1)} fusion(f32[256,8,88]{2,0,1:T(8,128)} %copy.50, f32[8,256]{1,0:T(8,128)S(1)} %add_rsqrt_fusion.2), kind=kLoop, calls=%fused_computation.46 | loop fusion | flops 360448 | bytes 1089536 | tf_op jit(solution)/shard_map/convert_element_type | solution.py:263
  86.0 49.5 %all-gather.3.cloned.1.call-done = bf16[128,256,88]{1,2,0:T(8,128)(2,1)} async-done(((bf16[2,256,88]{1,2,0:T(8,128)(2,1)}), bf16[128,256,88]{1,2,0:T(8,128)(2,1)}) %all-gather.3.cloned.1.call-update) | async-done | bytes 5767184 | tf_op jit(solution)/shard_map/all_gather | solution.py:271
  135.5 9.8 %copy.51 = bf16[128,256,88]{2,1,0:T(8,128)(2,1)} copy(bf16[128,256,88]{1,2,0:T(8,128)(2,1)} %all-gather.3.cloned.1.call-done) | data formatting | bytes 11534336 | tf_op jit(solution)/shard_map/all_gather | solution.py:271
  145.3 30.7 %shard_map.136 = bf16[8,256,88]{2,1,0:T(8,128)(2,1)} custom-call(s32[10]{0:T(128)} %constant.137.clone.query_block_ref, s32[10]{0:T(128)} %constant.138.clone.key_block_ref, s32[8]{0:T(128)} %pad_add_fusion.1.info_ref, bf16[8,256,88]{2,1,0:T(8,128)(2,1)} %fusion.34.q_ref, bf16[64,2,256,88]{3,2,1,0:T(8,128)(2,1)} %bitcast.121), custom_call_target="tpu_custom_call" | custom-call | tf_op jit(solution)/shard_map/pallas_call | solution.py:133
  176.1 1.2 copy.52
  177.3 1.3 collective-permute-start.4
  178.6 1.3 collective-permute-done.4
  179.9 4.4 %fusion.22 = bf16[256,1,1408]{2,0,1:T(8,128)(2,1)} fusion(bf16[1408,1408]{1,0:T(8,128)(2,1)} %maximum_select_fusion, bf16[256,1408]{1,0:T(8,128)(2,1)S(1)} %scatter_fusion, bf16[256,704]{0,1:T(8,128)(2,1)S(1)} %collective-permute-done.4, bf16[256,704]{0,1:T(8,128)(2,1)S(1)} %bitcast.128, pred[]{:T(512)S(6)} %eq.90), kind=kOutput, calls=%fused_computation.23 | convolution fusion | flops 1019346944 | bytes 6127617 | tf_op jit(solution)/shard_map/dot_general | solution.py:286
  (42 shorter events, 1.0 us)
Async XLA Ops:
  6.5 73.3 %copy-start = (bf16[1408,704]{0,1:T(8,128)(2,1)S(1)}, bf16[1408,704]{0,1:T(8,128)(2,1)}, u32[]{:S(2)}) copy-start(bf16[1408,704]{0,1:T(8,128)(2,1)} %param.23) | copy-start | bytes 5947396
  6.5 5.1 %copy-start.2 = (bf16[512,1408]{1,0:T(8,128)(2,1)S(1)}, bf16[512,1408]{1,0:T(8,128)(2,1)}, u32[]{:S(2)}) copy-start(bf16[512,1408]{1,0:T(8,128)(2,1)} %param.14) | copy-start | bytes 4325380
  6.5 20.7 %collective-permute-start.1 = (bf16[704,1408]{1,0:T(8,128)(2,1)}, bf16[704,1408]{1,0:T(8,128)(2,1)}, u32[]{:S(2)}, u32[]{:S(2)}) collective-permute-start(bf16[704,1408]{1,0:T(8,128)(2,1)} %param.21), channel_id=1, source_target_pairs={{0,64},{64,0},{1,65},{65,1},{2,66},{66,2},{3,67},{67,3},{4,68},{68... | collective-permute-start | bytes 5947400 | tf_op jit(solution)/shard_map/ppermute | solution.py:154
  23.2 1.4 copy-start.6
  24.4 2.8 %collective-permute-start = (bf16[256,704]{0,1:T(8,128)(2,1)}, bf16[256,704]{0,1:T(8,128)(2,1)}, u32[]{:S(2)}, u32[]{:S(2)}) collective-permute-start(bf16[256,704]{0,1:T(8,128)(2,1)} %convolution_convert_fusion), channel_id=1, source_target_pairs={{0,64},{64,0},{1,65},{65,1},{2,66},{66,2},{3,67},{67,3},{4,68},{68... | collective-permute-start | bytes 1081352 | tf_op jit(solution)/shard_map/ppermute | solution.py:154
  24.8 2.4 %copy-start.5 = (bf16[704,1408]{1,0:T(8,128)(2,1)S(1)}, bf16[704,1408]{1,0:T(8,128)(2,1)}, u32[]{:S(2)}) copy-start(bf16[704,1408]{1,0:T(8,128)(2,1)} %param.21) | copy-start | bytes 5947396
  30.5 5.2 %copy-start.4 = (s32[8192]{0:T(1024)S(1)}, s32[8192]{0:T(1024)}, u32[]{:S(2)}) copy-start(s32[8192]{0:T(1024)} %param.17) | copy-start | bytes 98308
  35.1 28.7 %copy-start.1 = (bf16[256,1,1408]{2,0,1:T(8,128)(2,1)S(1)}, bf16[256,1,1408]{2,0,1:T(8,128)(2,1)}, u32[]{:S(2)}) copy-start(bf16[256,1,1408]{2,0,1:T(8,128)(2,1)} %param.18) | copy-start | bytes 2162692
  35.1 3.2 %collective-permute-start.2 = (f32[128,1408]{1,0:T(8,128)S(1)}, f32[128,1408]{1,0:T(8,128)}, u32[]{:S(2)}, u32[]{:S(2)}) collective-permute-start(f32[128,1408]{1,0:T(8,128)S(1)} %fusion.77), channel_id=1, source_target_pairs={{0,64},{64,0},{1,65},{65,1},{2,66},{66,2},{3,67},{67,3},{4,68},{68... | collective-permute-start | bytes 2162696 | tf_op jit(solution)/shard_map/ppermute | solution.py:154
  41.6 22.1 %all-to-all-start = ((bf16[64,2,1408]{2,1,0:T(2,128)(2,1)}), bf16[64,2,1408]{2,1,0:T(2,128)(2,1)S(1)}, u32[]{:S(2)}, u32[]{:S(2)}) async-start(bf16[64,2,1408]{2,1,0:T(2,128)(2,1)} %fusion.56), calls=%async_computation | async-start | bytes 720896 | tf_op jit(solution)/shard_map/all_to_all | solution.py:240
  52.8 82.7 %all-gather.3.cloned.1.call-start = ((), (), s32[]{:S(2)}) async-start(), calls=%async_computation.1 | async-start | bytes 5857280 | tf_op jit(solution)/shard_map/all_gather | solution.py:271
  65.4 4.3 %copy-start.3 = (s32[256,64]{0,1:T(8,128)S(1)}, s32[256,64]{0,1:T(8,128)}, u32[]{:S(2)}) copy-start(s32[256,64]{0,1:T(8,128)} %param.19) | copy-start | bytes 196612
  67.9 5.7 %collective-permute-start.3 = (bf16[704,1408]{1,0:T(8,128)(2,1)}, bf16[704,1408]{1,0:T(8,128)(2,1)}, u32[]{:S(2)}, u32[]{:S(2)}) collective-permute-start(bf16[704,1408]{1,0:T(8,128)(2,1)} %param.25), channel_id=1, source_target_pairs={{0,64},{64,0},{1,65},{65,1},{2,66},{66,2},{3,67},{67,3},{4,68},{68... | collective-permute-start | bytes 5947400 | tf_op jit(solution)/shard_map/ppermute | solution.py:154
  177.3 2.6 %collective-permute-start.4 = (bf16[256,704]{0,1:T(8,128)(2,1)S(1)}, bf16[256,704]{0,1:T(8,128)(2,1)S(1)}, u32[]{:S(2)}, u32[]{:S(2)}) collective-permute-start(bf16[256,704]{0,1:T(8,128)(2,1)S(1)} %bitcast.127), channel_id=1, source_target_pairs={{0,64},{64,0},{1,65},{65,1},{2,66},{66,2},{3,67},{67,3},{4,68},{68... | collective-permute-start | bytes 1081352 | tf_op jit(solution)/shard_map/ppermute | solution.py:154
Sparse Core Ops, SparseCore 0:
  68.0 67.4 all-gather.2
where the time goes:
time: 192 us; the launch traced here: 191 us
  waiting for transfers between devices  64.6 us (34%)
  Pallas kernels  30.7 us (16%)
  matrix products  28.2 us (15%)
  other arithmetic  18.7 us (10%)
  local copies, waits for them, and re-layouts  16.7 us (9%)
  starting transfers between devices  16.5 us (9%)
  between operations  15.7 us (8%)
    all_gather x1, waiting for transfers between devices, body(): piece = lax.all_gather(shared, 'seq', axis=0, tiled=True)  49.5 us
    pallas_call x1, Pallas kernels, text_attention(): pl.pallas_call(functools.partial(_text_kernel, scale=scale), grid_spec=pl...  30.7 us
    all_to_all x1, starting transfers between devices, body(): lax.all_to_all(jnp.transpose(jnp.roll(image_rows.reshape(per_peer, seq_co...  11.2 us
    all_to_all x1, waiting for transfers between devices, body(): lax.all_to_all(jnp.transpose(jnp.roll(image_rows.reshape(per_peer, seq_co...  10.6 us
    all_gather x1, local copies, waits for them, and re-layouts, body(): piece = lax.all_gather(shared, 'seq', axis=0, tiled=True)  9.83 us
    select_n x1, other arithmetic, in_head_order(): jnp.where(first, jnp.concatenate([own, other], axis), jnp.concatenate([ot...  6.23 us
    dot_general x1, matrix products, body(): jnp.dot(normed, vision_qkv.reshape(D, -1), preferred_element_type=jnp.flo...  5.99 us
    ppermute x5, starting transfers between devices, swap(): return lax.ppermute(values, 'section', [(0, 1), (1, 0)])  5.26 us
  transfers between devices with their start and end apart: 7, of which 4 were waited for; matrix products, arithmetic and copies ran while one was open for 17% of the time, Pallas kernels for 0%

commit v1 on v0

--- a/solution.py
+++ b/solution.py
@@ -209,7 +209,14 @@
         .astype(jnp.bfloat16)
         .reshape(patch_count, local_heads * HEAD)
     )
-    picks = merge_rows(image_grid, offsets, merged_count)
+    per_peer = merged_count // seq_count
+    run_starts = dest_positions.reshape(seq_count, merged_count)[:, 0]
+    own_start = run_starts[seq_index]
+    send_order = (
+        jnp.arange(per_peer, dtype=jnp.int32)[None, :] * seq_count
+        + (jnp.arange(seq_count, dtype=jnp.int32)[:, None] - own_start) % seq_count
+    ).reshape(-1)
+    picks = merge_rows(image_grid, offsets, merged_count)[send_order]
     own_picks = lax.dynamic_slice_in_dim(picks, 2 * section_index, 2, 1).reshape(-1)
     other_picks = lax.dynamic_slice_in_dim(picks, 2 - 2 * section_index, 2, 1).reshape(-1)
     patch_ids = jnp.arange(patch_count, dtype=jnp.int32)[None, :]
@@ -227,20 +234,16 @@
         jnp.dot(own_select, patches, preferred_element_type=jnp.float32)
         + jnp.dot(own_rows, full_out, preferred_element_type=jnp.float32)
     ).astype(jnp.bfloat16)
-    merge_terms = jnp.dot(
-        kept.reshape(merged_count, 2 * D),
-        projector.reshape(2 * D, D),
-        preferred_element_type=jnp.float32,
-    )
-    image_rows = (merge_terms + swap(merge_terms)).astype(jnp.bfloat16)
-
-    per_peer = merged_count // seq_count
-    run_starts = dest_positions.reshape(seq_count, merged_count)[:, 0]
-    own_start = run_starts[seq_index]
+    halves = []
+    for half in jnp.split(kept.reshape(merged_count, 2 * D), 2):
+        merge_terms = jnp.dot(
+            half, projector.reshape(2 * D, D), preferred_element_type=jnp.float32
+        )
+        halves.append((merge_terms + swap(merge_terms)).astype(jnp.bfloat16))
+    image_rows = jnp.concatenate(halves)
+
     received = lax.all_to_all(
-        jnp.transpose(
-            jnp.roll(image_rows.reshape(per_peer, seq_count, D), own_start, axis=1), (1, 0, 2)
-        ),
+        image_rows.reshape(seq_count, per_peer, D),
         "seq",
         split_axis=0,
         concat_axis=0,

time: 192 us -> 205 us (1.068)
  matrix products: 28.2 us -> 36.1 us
  local copies, waits for them, and re-layouts: 16.7 us -> 22.3 us
  Pallas kernels: 30.7 us -> 27.5 us
    dot_general x1 -> x2, matrix products: 4.54 us -> 9.44 us  [body(): jnp.dot(half, projector.reshape(2 * D, D), preferred_element_type=jnp.flo...]
    pallas_call x1, Pallas kernels: 30.7 us -> 27.5 us  [text_attention(): pl.pallas_call(functools.partial(_text_kernel, scale=scale), grid_spec=pl...]
    ppermute x5 -> x6, waiting for transfers between devices: 4.52 us -> 5.99 us  [swap(): return lax.ppermute(values, 'section', [(0, 1), (1, 0)])]
    ppermute x5 -> x6, starting transfers between devices: 5.26 us -> 5.52 us  [swap(): return lax.ppermute(values, 'section', [(0, 1), (1, 0)])]
  transfers between devices with their start and end apart: 7 -> 8, of which waited for: 4 -> 5; matrix products, arithmetic and copies ran while one was open for 17% -> 24% of each run, Pallas kernels for 0% -> 0%
where the time goes in v1:
time: 205 us; the launch traced here: 202 us
  waiting for transfers between devices  66.2 us (32%)
  matrix products  36.1 us (18%)
  Pallas kernels  27.5 us (13%)
  local copies, waits for them, and re-layouts  22.3 us (11%)
  other arithmetic  19.8 us (10%)
  starting transfers between devices  16.8 us (8%)
  between operations  13.7 us (7%)
    all_gather x1, waiting for transfers between devices, body(): piece = lax.all_gather(shared, 'seq', axis=0, tiled=True)  49.5 us
    pallas_call x1, Pallas kernels, text_attention(): pl.pallas_call(functools.partial(_text_kernel, scale=scale), grid_spec=pl...  27.5 us
    all_to_all x1, starting transfers between devices, body(): lax.all_to_all(image_rows.reshape(seq_count, per_peer, D), 'seq', split_a...  11.2 us
    all_to_all x1, waiting for transfers between devices, body(): lax.all_to_all(image_rows.reshape(seq_count, per_peer, D), 'seq', split_a...  10.6 us
    all_gather x1, local copies, waits for them, and re-layouts, body(): piece = lax.all_gather(shared, 'seq', axis=0, tiled=True)  9.83 us
    dot_general x2, matrix products, body(): jnp.dot(half, projector.reshape(2 * D, D), preferred_element_type=jnp.flo...  9.44 us
    select_n x1, other arithmetic, in_head_order(): jnp.where(first, jnp.concatenate([own, other], axis), jnp.concatenate([ot...  6.23 us
    ppermute x6, waiting for transfers between devices, swap(): return lax.ppermute(values, 'section', [(0, 1), (1, 0)])  5.99 us
  transfers between devices with their start and end apart: 8, of which 5 were waited for; matrix products, arithmetic and copies ran while one was open for 24% of the time, Pallas kernels for 0%

profile of v1, /device:TPU:1, one launch (start us, length us, event | category | flops | bytes accessed | tf_op | source)
XLA Modules:
  0.0 202.4 jit_solution(15367053998469028440)
XLA Ops:
  6.5 1.4 collective-permute-start.1
  8.0 0.7 slice_bitcast_fusion.2
  8.6 0.8 fusion.70
  9.9 0.9 fusion.77
  10.7 0.5 constant_dynamic-slice_fusion.2
  11.3 0.7 and_select_fusion
  11.9 0.7 broadcast_add_fusion
  12.8 0.6 pad_clamp_fusion
  13.4 1.6 convert_reduce_fusion
  15.5 6.0 %fusion.29 = f32[512,3,8,88]{0,3,2,1:T(8,128)S(1)} fusion(bf16[3,8,88,1408]{3,2,1,0:T(8,128)(2,1)} %bitcast.131, bf16[512,1408]{1,0:T(8,128)(2,1)S(1)} %copy-done.2, f32[512]{0:T(512)S(1)} %add_rsqrt_fusion.3, f32[512]{0:T(512)S(1)} %broadcast_multiply_fusion), kind=kOutput, calls=%fused_computation.31 | convolution fusion | flops 3047948288 | bytes 11718656 | tf_op jit(solution)/shard_map/dot_general | solution.py:190
  21.5 2.0 copy-done.3
  23.5 1.0 multiply_reduce_fusion.1
  24.5 0.9 broadcast_compare_fusion
  25.4 0.8 gather_fusion
  26.2 0.7 constant_dynamic-slice_fusion
  26.9 1.0 eq.85
  27.9 0.8 add_rsqrt_fusion
  28.6 4.2 %fusion = (f32[8,512]{1,0:T(8,128)S(1)}, f32[8,512,512]{1,2,0:T(8,128)S(1)}) fusion(pred[512,512]{0,1:T(8,128)(4,1)} %broadcast_compare_fusion, f32[512,3,8,88]{0,3,2,1:T(8,128)} %copy-done.3, f32[512,8]{0,1:T(8,128)S(1)} %get-tuple-element.33, f32[512,8]{0,1:T(8,128)S(1)} %get-tuple-element.34), kind=kOutput, calls=%fused_computation.3 | convolution fusion | flops 376827904 | bytes 11583488 | tf_op jit(solution)/shard_map/qhd,khd->hqk/dot_general | solution.py:200
  32.9 3.1 %divide_convert_fusion = bf16[512,8,88]{0,2,1:T(8,128)(2,1)S(1)} fusion(f32[8,512,512]{1,2,0:T(8,128)S(1)} %get-tuple-element.30, pred[512,512]{0,1:T(8,128)(4,1)S(1)} %copy-done.4, f32[512,3,8,88]{0,3,2,1:T(8,128)} %copy-done.3, f32[512,8]{0,1:T(8,128)S(1)} %bitcast.134), kind=kOutput, calls=%fused_computation.35 | convolution fusion | flops 376111104 | bytes 10108928 | tf_op jit(solution)/shard_map/hqk,khd->qhd/dot_general | solution.py:204
  36.0 1.2 convolution_convert_fusion
  37.6 1.7 convolution_convert_fusion.1
  39.3 0.6 fusion.53
  39.9 3.1 %fusion.19 = bf16[256,1408]{1,0:T(8,128)(2,1)S(1)} fusion(f32[256,1408]{1,0:T(8,128)S(1)} %fusion.53, bf16[704,1408]{1,0:T(8,128)(2,1)} %collective-permute-done.1, bf16[704,1408]{1,0:T(8,128)(2,1)S(1)} %copy-done.7, bf16[256,704]{0,1:T(8,128)(2,1)} %collective-permute-done, bf16[256,704]{0,1:T(8,128)(2,1)S(1)} %convolution_convert_fusion.1), kind=kOutput, calls=%fused_computation.23 | convolution fusion | flops 1025114112 | bytes 6848512 | tf_op jit(solution)/shard_map/dot_general | solution.py:235
  43.2 4.7 %fusion.78 = f32[64,1408]{1,0:T(8,128)S(1)} fusion(bf16[64,2816]{1,0:T(8,128)(2,1)S(1)} %split.11, bf16[2816,1408]{1,0:T(8,128)(2,1)} %bitcast.122), kind=kOutput, calls=%fused_computation.158 | convolution fusion | flops 507510784 | bytes 8650752 | tf_op jit(solution)/shard_map/dot_general | solution.py:239
  47.9 0.6 collective-permute-start.2
  48.6 4.7 %fusion.79 = f32[64,1408]{1,0:T(8,128)S(1)} fusion(bf16[64,2816]{1,0:T(8,128)(2,1)S(1)} %split.13, bf16[2816,1408]{1,0:T(8,128)(2,1)} %bitcast.123), kind=kOutput, calls=%fused_computation.159 | convolution fusion | flops 507510784 | bytes 8650752 | tf_op jit(solution)/shard_map/dot_general | solution.py:239
  53.7 1.5 collective-permute-done.3
  55.2 0.9 reshape.540
  56.1 11.2 %all-to-all-start = ((bf16[64,2,1408]{2,1,0:T(2,128)(2,1)}), bf16[64,2,1408]{2,1,0:T(2,128)(2,1)S(1)}, u32[]{:S(2)}, u32[]{:S(2)}) async-start(bf16[64,2,1408]{2,1,0:T(2,128)(2,1)} %reshape.540), calls=%async_computation | async-start | bytes 720896 | tf_op jit(solution)/shard_map/all_to_all | solution.py:245
  67.5 10.6 %all-to-all-done = bf16[64,2,1408]{2,1,0:T(2,128)(2,1)S(1)} async-done(((bf16[64,2,1408]{2,1,0:T(2,128)(2,1)}), bf16[64,2,1408]{2,1,0:T(2,128)(2,1)S(1)}, u32[]{:S(2)}, u32[]{:S(2)}) %all-to-all-start) | async-done | bytes 360480 | tf_op jit(solution)/shard_map/all_to_all | solution.py:245
  78.3 1.6 scatter_fusion
  80.1 1.5 fusion.48
  81.7 0.7 pad_maximum_fusion.1
  82.4 1.8 collective-permute-start.4
  84.4 0.6 pad_add_fusion.1.info_ref
  84.9 3.2 %collective-permute-done.4 = bf16[704,1408]{1,0:T(8,128)(2,1)} collective-permute-done((bf16[704,1408]{1,0:T(8,128)(2,1)}, bf16[704,1408]{1,0:T(8,128)(2,1)}, u32[]{:S(2)}, u32[]{:S(2)}) %collective-permute-start.4) | collective-permute-done | bytes 1982496 | tf_op jit(solution)/shard_map/ppermute | solution.py:154
  88.1 6.2 %maximum_select_fusion = bf16[1408,1408]{1,0:T(8,128)(2,1)} fusion(bf16[704,1408]{1,0:T(8,128)(2,1)} %collective-permute-done.4, bf16[704,1408]{1,0:T(8,128)(2,1)} %param.25, pred[]{:T(512)S(6)} %eq.89), kind=kLoop, calls=%fused_computation.13 | loop fusion | flops 17842176 | bytes 7929857 | tf_op jit(solution)/shard_map/jit(_where)/select_n | solution.py:158
  94.4 0.8 fusion.56
  95.2 1.3 copy.82
  96.5 1.6 fusion.33
  98.1 2.4 %fusion.34.q_ref = bf16[8,256,88]{2,1,0:T(8,128)(2,1)} fusion(f32[256,8,88]{2,0,1:T(8,128)} %copy.82, f32[8,256]{1,0:T(8,128)S(1)} %add_rsqrt_fusion.2), kind=kLoop, calls=%fused_computation.47 | loop fusion | flops 360448 | bytes 1089536 | tf_op jit(solution)/shard_map/convert_element_type | solution.py:266
  100.5 49.5 %all-gather.3.cloned.1.call-done = bf16[128,256,88]{1,2,0:T(8,128)(2,1)} async-done(((bf16[2,256,88]{1,2,0:T(8,128)(2,1)}), bf16[128,256,88]{1,2,0:T(8,128)(2,1)}) %all-gather.3.cloned.1.call-update) | async-done | bytes 5767184 | tf_op jit(solution)/shard_map/all_gather | solution.py:274
  150.0 9.8 %copy.83 = bf16[128,256,88]{2,1,0:T(8,128)(2,1)} copy(bf16[128,256,88]{1,2,0:T(8,128)(2,1)} %all-gather.3.cloned.1.call-done) | data formatting | bytes 11534336 | tf_op jit(solution)/shard_map/all_gather | solution.py:274
  159.8 27.5 %shard_map.136 = bf16[8,256,88]{2,1,0:T(8,128)(2,1)} custom-call(s32[10]{0:T(128)} %constant.132.clone.query_block_ref, s32[10]{0:T(128)} %constant.133.clone.key_block_ref, s32[8]{0:T(128)} %pad_add_fusion.1.info_ref, bf16[8,256,88]{2,1,0:T(8,128)(2,1)} %fusion.34.q_ref, bf16[64,2,256,88]{3,2,1,0:T(8,128)(2,1)} %bitcast.124), custom_call_target="tpu_custom_call" | custom-call | tf_op jit(solution)/shard_map/pallas_call | solution.py:133
  187.3 1.2 copy.84
  188.6 1.3 collective-permute-start.5
  189.9 1.3 collective-permute-done.5
  191.2 4.4 %fusion.22 = bf16[256,1,1408]{2,0,1:T(8,128)(2,1)} fusion(bf16[1408,1408]{1,0:T(8,128)(2,1)} %maximum_select_fusion, bf16[256,1408]{1,0:T(8,128)(2,1)S(1)} %scatter_fusion, bf16[256,704]{0,1:T(8,128)(2,1)S(1)} %collective-permute-done.5, bf16[256,704]{0,1:T(8,128)(2,1)S(1)} %bitcast.129, pred[]{:T(512)S(6)} %eq.89), kind=kOutput, calls=%fused_computation.24 | convolution fusion | flops 1019346944 | bytes 6127617 | tf_op jit(solution)/shard_map/dot_general | solution.py:289
  (55 shorter events, 2.9 us)
Async XLA Ops:
  6.5 87.8 %copy-start = (bf16[1408,704]{0,1:T(8,128)(2,1)S(1)}, bf16[1408,704]{0,1:T(8,128)(2,1)}, u32[]{:S(2)}) copy-start(bf16[1408,704]{0,1:T(8,128)(2,1)} %param.23) | copy-start | bytes 5947396
  6.5 8.5 %copy-start.2 = (bf16[512,1408]{1,0:T(8,128)(2,1)S(1)}, bf16[512,1408]{1,0:T(8,128)(2,1)}, u32[]{:S(2)}) copy-start(bf16[512,1408]{1,0:T(8,128)(2,1)} %param.14) | copy-start | bytes 4325380
  6.5 33.4 %collective-permute-start.1 = (bf16[704,1408]{1,0:T(8,128)(2,1)}, bf16[704,1408]{1,0:T(8,128)(2,1)}, u32[]{:S(2)}, u32[]{:S(2)}) collective-permute-start(bf16[704,1408]{1,0:T(8,128)(2,1)} %param.21), channel_id=1, source_target_pairs={{0,64},{64,0},{1,65},{65,1},{2,66},{66,2},{3,67},{67,3},{4,68},{68... | collective-permute-start | bytes 5947400 | tf_op jit(solution)/shard_map/ppermute | solution.py:154
  21.5 2.0 copy-start.3
  28.6 4.2 %copy-start.4 = (pred[512,512]{0,1:T(8,128)(4,1)S(1)}, pred[512,512]{0,1:T(8,128)(4,1)}, u32[]{:S(2)}) copy-start(pred[512,512]{0,1:T(8,128)(4,1)} %broadcast_compare_fusion) | copy-start | bytes 786436
  36.0 1.4 copy-start.8
  37.2 2.7 %collective-permute-start = (bf16[256,704]{0,1:T(8,128)(2,1)}, bf16[256,704]{0,1:T(8,128)(2,1)}, u32[]{:S(2)}, u32[]{:S(2)}) collective-permute-start(bf16[256,704]{0,1:T(8,128)(2,1)} %convolution_convert_fusion), channel_id=1, source_target_pairs={{0,64},{64,0},{1,65},{65,1},{2,66},{66,2},{3,67},{67,3},{4,68},{68... | collective-permute-start | bytes 1081352 | tf_op jit(solution)/shard_map/ppermute | solution.py:154
  37.5 2.4 %copy-start.7 = (bf16[704,1408]{1,0:T(8,128)(2,1)S(1)}, bf16[704,1408]{1,0:T(8,128)(2,1)}, u32[]{:S(2)}) copy-start(bf16[704,1408]{1,0:T(8,128)(2,1)} %param.21) | copy-start | bytes 5947396
  47.9 5.7 %collective-permute-start.2 = (f32[64,1408]{1,0:T(8,128)S(1)}, f32[64,1408]{1,0:T(8,128)S(1)}, u32[]{:S(2)}, u32[]{:S(2)}) collective-permute-start(f32[64,1408]{1,0:T(8,128)S(1)} %fusion.78), channel_id=1, source_target_pairs={{0,64},{64,0},{1,65},{65,1},{2,66},{66,2},{3,67},{67,3},{4,68},{68... | collective-permute-start | bytes 1081352 | tf_op jit(solution)/shard_map/ppermute | solution.py:154
  53.4 14.0 %copy-start.5 = (s32[64,2]{1,0:T(8,128)S(1)}, s32[64,2]{1,0:T(8,128)}, u32[]{:S(2)}) copy-start(s32[64,2]{1,0:T(8,128)} %get-tuple-element.28) | copy-start | bytes 1540
  53.4 24.9 %copy-start.1 = (bf16[256,1,1408]{2,0,1:T(8,128)(2,1)S(1)}, bf16[256,1,1408]{2,0,1:T(8,128)(2,1)}, u32[]{:S(2)}) copy-start(bf16[256,1,1408]{2,0,1:T(8,128)(2,1)} %param.18) | copy-start | bytes 2162692
  53.4 1.8 collective-permute-start.3
  56.1 22.1 %all-to-all-start = ((bf16[64,2,1408]{2,1,0:T(2,128)(2,1)}), bf16[64,2,1408]{2,1,0:T(2,128)(2,1)S(1)}, u32[]{:S(2)}, u32[]{:S(2)}) async-start(bf16[64,2,1408]{2,1,0:T(2,128)(2,1)} %reshape.540), calls=%async_computation | async-start | bytes 720896 | tf_op jit(solution)/shard_map/all_to_all | solution.py:245
  67.3 82.7 %all-gather.3.cloned.1.call-start = ((), (), s32[]{:S(2)}) async-start(), calls=%async_computation.1 | async-start | bytes 5857280 | tf_op jit(solution)/shard_map/all_gather | solution.py:274
  79.9 4.3 %copy-start.6 = (s32[256,64]{0,1:T(8,128)S(1)}, s32[256,64]{0,1:T(8,128)}, u32[]{:S(2)}) copy-start(s32[256,64]{0,1:T(8,128)} %param.19) | copy-start | bytes 196612
  82.4 5.7 %collective-permute-start.4 = (bf16[704,1408]{1,0:T(8,128)(2,1)}, bf16[704,1408]{1,0:T(8,128)(2,1)}, u32[]{:S(2)}, u32[]{:S(2)}) collective-permute-start(bf16[704,1408]{1,0:T(8,128)(2,1)} %param.25), channel_id=1, source_target_pairs={{0,64},{64,0},{1,65},{65,1},{2,66},{66,2},{3,67},{67,3},{4,68},{68... | collective-permute-start | bytes 5947400 | tf_op jit(solution)/shard_map/ppermute | solution.py:154
  188.6 2.6 %collective-permute-start.5 = (bf16[256,704]{0,1:T(8,128)(2,1)S(1)}, bf16[256,704]{0,1:T(8,128)(2,1)S(1)}, u32[]{:S(2)}, u32[]{:S(2)}) collective-permute-start(bf16[256,704]{0,1:T(8,128)(2,1)S(1)} %bitcast.128), channel_id=1, source_target_pairs={{0,64},{64,0},{1,65},{65,1},{2,66},{66,2},{3,67},{67,3},{4,68},{68... | collective-permute-start | bytes 1081352 | tf_op jit(solution)/shard_map/ppermute | solution.py:154
Sparse Core Ops, SparseCore 0:
  82.5 67.4 all-gather.2

commit v2 on v0

--- a/solution.py
+++ b/solution.py
@@ -281,9 +281,13 @@
         (in_head_order(first, decoder_out, decoder_out_other, 0), head_queries)
     )
     head_major = text_attention(info, head_queries, piece, rows, scale)
-    attended_text = jnp.transpose(head_major, (1, 0, 2)).reshape(text_rows, -1)
-    all_heads = in_head_order(first, attended_text, swap(attended_text), 1)
-    output_terms = jnp.dot(all_heads, decoder_out_full, preferred_element_type=jnp.float32)
+    all_heads = in_head_order(first, head_major, swap(head_major), 0)
+    output_terms = jnp.einsum(
+        "hte,hed->td",
+        all_heads,
+        decoder_out_full.reshape(2 * local_heads, HEAD, D),
+        preferred_element_type=jnp.float32,
+    )
     decoded = (prompt.astype(jnp.float32) + output_terms).astype(jnp.bfloat16)
     return decoded.reshape(text_rows, 1, D)
 

time: 192 us -> 191 us (level)
  no operation moved by 1% of the time
where the time goes in v2:
time: 191 us; the launch traced here: 190 us
  waiting for transfers between devices  65.1 us (34%)
  Pallas kernels  30.1 us (16%)
  matrix products  28.8 us (15%)
  other arithmetic  18.7 us (10%)
  starting transfers between devices  16.5 us (9%)
  between operations  15.7 us (8%)
  local copies, waits for them, and re-layouts  15.5 us (8%)
    all_gather x1, waiting for transfers between devices, body(): piece = lax.all_gather(shared, 'seq', axis=0, tiled=True)  49.5 us
    pallas_call x1, Pallas kernels, text_attention(): pl.pallas_call(functools.partial(_text_kernel, scale=scale), grid_spec=pl...  30.1 us
    all_to_all x1, starting transfers between devices, body(): lax.all_to_all(jnp.transpose(jnp.roll(image_rows.reshape(per_peer, seq_co...  11.2 us
    all_to_all x1, waiting for transfers between devices, body(): lax.all_to_all(jnp.transpose(jnp.roll(image_rows.reshape(per_peer, seq_co...  10.6 us
    all_gather x1, local copies, waits for them, and re-layouts, body(): piece = lax.all_gather(shared, 'seq', axis=0, tiled=True)  9.83 us
    select_n x1, other arithmetic, in_head_order(): jnp.where(first, jnp.concatenate([own, other], axis), jnp.concatenate([ot...  6.23 us
    dot_general x1, matrix products, body(): jnp.dot(normed, vision_qkv.reshape(D, -1), preferred_element_type=jnp.flo...  5.99 us
    ppermute x5, starting transfers between devices, swap(): return lax.ppermute(values, 'section', [(0, 1), (1, 0)])  5.18 us
  transfers between devices with their start and end apart: 7, of which 4 were waited for; matrix products, arithmetic and copies ran while one was open for 17% of the time, Pallas kernels for 0%

profile of v2, /device:TPU:1, one launch (start us, length us, event | category | flops | bytes accessed | tf_op | source)
XLA Modules:
  0.0 190.3 jit_solution(4633277887245932140)
XLA Ops:
  6.5 1.4 collective-permute-start.1
  8.0 0.7 slice_bitcast_fusion.2
  8.6 0.8 fusion.71
  9.6 0.1 broadcast_add_fusion.1
  9.9 0.1 eq.86
  10.0 1.6 convert_reduce_fusion
  11.7 0.5 fusion.13
  12.2 6.0 %fusion.30 = f32[512,3,8,88]{0,3,2,1:T(8,128)S(1)} fusion(bf16[3,8,88,1408]{3,2,1,0:T(8,128)(2,1)} %bitcast.135, bf16[512,1408]{1,0:T(8,128)(2,1)S(1)} %copy-done.2, f32[512]{0:T(512)S(1)} %add_rsqrt_fusion.3, f32[512]{0:T(512)S(1)} %broadcast_multiply_fusion), kind=kOutput, calls=%fused_computation.31 | convolution fusion | flops 3047948288 | bytes 11718656 | tf_op jit(solution)/shard_map/dot_general | solution.py:190
  18.2 0.4 multiply_reduce_fusion.1
  18.6 0.2 broadcast_compare_fusion
  18.9 2.5 %fusion = (f32[8,512]{1,0:T(8,128)S(1)}, f32[8,512,512]{1,2,0:T(8,128)S(1)}) fusion(pred[512,512]{0,1:T(8,128)(4,1)S(1)} %broadcast_compare_fusion, f32[512,3,8,88]{0,3,2,1:T(8,128)S(1)} %fusion.30, f32[512,8]{0,1:T(8,128)S(1)} %get-tuple-element.27, f32[512,8]{0,1:T(8,128)S(1)} %get-tuple-element.28), kind=kOutput, calls=%fused_computation.2 | convolution fusion | flops 376827904 | bytes 11583488 | tf_op jit(solution)/shard_map/qhd,khd->hqk/dot_general | solution.py:200
  21.4 1.8 divide_convert_fusion
  23.2 1.2 convolution_convert_fusion
  24.4 0.2 collective-permute-start
  24.7 0.1 eq.79
  24.8 1.7 convolution_convert_fusion.1
  26.6 0.6 fusion.54
  27.2 3.1 %fusion.20 = bf16[256,1408]{1,0:T(8,128)(2,1)S(1)} fusion(f32[256,1408]{1,0:T(8,128)S(1)} %fusion.54, bf16[704,1408]{1,0:T(8,128)(2,1)} %collective-permute-done.1, bf16[704,1408]{1,0:T(8,128)(2,1)S(1)} %copy-done.5, bf16[256,704]{0,1:T(8,128)(2,1)} %collective-permute-done, bf16[256,704]{0,1:T(8,128)(2,1)S(1)} %convolution_convert_fusion.1), kind=kOutput, calls=%fused_computation.23 | convolution fusion | flops 1025114112 | bytes 6848512 | tf_op jit(solution)/shard_map/dot_general | solution.py:228
  30.3 0.2 reshape.479
  30.6 4.5 %fusion.78 = f32[128,1408]{1,0:T(8,128)S(1)} fusion(bf16[128,2816]{1,0:T(8,128)(2,1)S(1)} %reshape.479, bf16[2816,1408]{1,0:T(8,128)(2,1)} %bitcast.129), kind=kOutput, calls=%fused_computation.151 | convolution fusion | flops 1015021568 | bytes 9371648 | tf_op jit(solution)/shard_map/dot_general | solution.py:230
  35.1 0.6 collective-permute-start.2
  35.8 0.5 constant_dynamic-slice_fusion
  38.3 1.2 add_convert_fusion
  39.5 0.4 copy.49
  39.9 1.7 fusion.57
  41.6 11.2 %all-to-all-start = ((bf16[64,2,1408]{2,1,0:T(2,128)(2,1)}), bf16[64,2,1408]{2,1,0:T(2,128)(2,1)S(1)}, u32[]{:S(2)}, u32[]{:S(2)}) async-start(bf16[64,2,1408]{2,1,0:T(2,128)(2,1)} %fusion.57), calls=%async_computation | async-start | bytes 720896 | tf_op jit(solution)/shard_map/all_to_all | solution.py:240
  52.9 0.1 add.316
  53.1 10.6 %all-to-all-done = bf16[64,2,1408]{2,1,0:T(2,128)(2,1)S(1)} async-done(((bf16[64,2,1408]{2,1,0:T(2,128)(2,1)}), bf16[64,2,1408]{2,1,0:T(2,128)(2,1)S(1)}, u32[]{:S(2)}, u32[]{:S(2)}) %all-to-all-start) | async-done | bytes 360480 | tf_op jit(solution)/shard_map/all_to_all | solution.py:240
  63.7 0.1 reshape.491
  63.8 1.6 scatter_fusion
  65.4 0.2 fusion.27
  65.6 1.5 fusion.50
  67.2 0.7 pad_maximum_fusion
  67.9 1.8 collective-permute-start.3
  69.7 0.2 convert_reduce_fusion.1
  69.8 0.6 pad_add_fusion.1.info_ref
  70.4 3.2 %collective-permute-done.3 = bf16[704,1408]{1,0:T(8,128)(2,1)} collective-permute-done((bf16[704,1408]{1,0:T(8,128)(2,1)}, bf16[704,1408]{1,0:T(8,128)(2,1)}, u32[]{:S(2)}, u32[]{:S(2)}) %collective-permute-start.3) | collective-permute-done | bytes 1982496 | tf_op jit(solution)/shard_map/ppermute | solution.py:154
  73.6 6.2 %maximum_select_fusion = bf16[1408,1408]{1,0:T(8,128)(2,1)} fusion(bf16[704,1408]{1,0:T(8,128)(2,1)} %collective-permute-done.3, bf16[704,1408]{1,0:T(8,128)(2,1)} %param.25, pred[]{:T(512)S(6)} %eq.90), kind=kLoop, calls=%fused_computation.12 | loop fusion | flops 17842176 | bytes 7929857 | tf_op jit(solution)/shard_map/jit(_where)/select_n | solution.py:158
  79.9 0.8 fusion.59
  80.7 1.3 copy.51
  82.0 1.6 fusion.39
  83.6 2.4 %fusion.40.q_ref = bf16[8,256,88]{2,1,0:T(8,128)(2,1)} fusion(f32[256,8,88]{2,0,1:T(8,128)} %copy.51, f32[8,256]{1,0:T(8,128)S(1)} %add_rsqrt_fusion.2), kind=kLoop, calls=%fused_computation.53 | loop fusion | flops 360448 | bytes 1089536 | tf_op jit(solution)/shard_map/convert_element_type | solution.py:263
  86.0 49.5 %all-gather.3.cloned.1.call-done = bf16[128,256,88]{1,2,0:T(8,128)(2,1)} async-done(((bf16[2,256,88]{1,2,0:T(8,128)(2,1)}), bf16[128,256,88]{1,2,0:T(8,128)(2,1)}) %all-gather.3.cloned.1.call-update) | async-done | bytes 5767184 | tf_op jit(solution)/shard_map/all_gather | solution.py:271
  135.5 9.8 %copy.52 = bf16[128,256,88]{2,1,0:T(8,128)(2,1)} copy(bf16[128,256,88]{1,2,0:T(8,128)(2,1)} %all-gather.3.cloned.1.call-done) | data formatting | bytes 11534336 | tf_op jit(solution)/shard_map/all_gather | solution.py:271
  145.3 30.1 %shard_map.136 = bf16[8,256,88]{2,1,0:T(8,128)(2,1)} custom-call(s32[10]{0:T(128)} %constant.137.clone.query_block_ref, s32[10]{0:T(128)} %constant.138.clone.key_block_ref, s32[8]{0:T(128)} %pad_add_fusion.1.info_ref, bf16[8,256,88]{2,1,0:T(8,128)(2,1)} %fusion.40.q_ref, bf16[64,2,256,88]{3,2,1,0:T(8,128)(2,1)} %bitcast.128), custom_call_target="tpu_custom_call" | custom-call | tf_op jit(solution)/shard_map/pallas_call | solution.py:133
  175.5 1.2 collective-permute-start.4
  176.7 1.7 collective-permute-done.4
  178.4 5.1 %fusion.23 = bf16[256,1,1408]{2,0,1:T(8,128)(2,1)} fusion(bf16[16,88,1408]{2,1,0:T(8,128)(2,1)} %bitcast.131, bf16[256,1408]{1,0:T(8,128)(2,1)S(1)} %scatter_fusion, bf16[8,256,88]{2,1,0:T(8,128)(2,1)S(1)} %collective-permute-done.4, bf16[8,256,88]{2,1,0:T(8,128)(2,1)} %shard_map.136, pred[]{:T(512)S(6)} %eq.90), kind=kOutput, calls=%fused_computation.24 | convolution fusion | flops 1017184256 | bytes 6127617 | tf_op jit(solution)/shard_map/hte,hed->td/dot_general | solution.py:285
  (41 shorter events, 0.8 us)
Async XLA Ops:
  6.5 73.3 %copy-start = (bf16[1408,704]{0,1:T(8,128)(2,1)S(1)}, bf16[1408,704]{0,1:T(8,128)(2,1)}, u32[]{:S(2)}) copy-start(bf16[1408,704]{0,1:T(8,128)(2,1)} %param.23) | copy-start | bytes 5947396
  6.5 5.1 %copy-start.2 = (bf16[512,1408]{1,0:T(8,128)(2,1)S(1)}, bf16[512,1408]{1,0:T(8,128)(2,1)}, u32[]{:S(2)}) copy-start(bf16[512,1408]{1,0:T(8,128)(2,1)} %param.14) | copy-start | bytes 4325380
  6.5 20.7 %collective-permute-start.1 = (bf16[704,1408]{1,0:T(8,128)(2,1)}, bf16[704,1408]{1,0:T(8,128)(2,1)}, u32[]{:S(2)}, u32[]{:S(2)}) collective-permute-start(bf16[704,1408]{1,0:T(8,128)(2,1)} %param.21), channel_id=1, source_target_pairs={{0,64},{64,0},{1,65},{65,1},{2,66},{66,2},{3,67},{67,3},{4,68},{68... | collective-permute-start | bytes 5947400 | tf_op jit(solution)/shard_map/ppermute | solution.py:154
  23.2 1.4 copy-start.6
  24.4 2.8 %collective-permute-start = (bf16[256,704]{0,1:T(8,128)(2,1)}, bf16[256,704]{0,1:T(8,128)(2,1)}, u32[]{:S(2)}, u32[]{:S(2)}) collective-permute-start(bf16[256,704]{0,1:T(8,128)(2,1)} %convolution_convert_fusion), channel_id=1, source_target_pairs={{0,64},{64,0},{1,65},{65,1},{2,66},{66,2},{3,67},{67,3},{4,68},{68... | collective-permute-start | bytes 1081352 | tf_op jit(solution)/shard_map/ppermute | solution.py:154
  24.8 2.4 %copy-start.5 = (bf16[704,1408]{1,0:T(8,128)(2,1)S(1)}, bf16[704,1408]{1,0:T(8,128)(2,1)}, u32[]{:S(2)}) copy-start(bf16[704,1408]{1,0:T(8,128)(2,1)} %param.21) | copy-start | bytes 5947396
  30.5 5.2 %copy-start.4 = (s32[8192]{0:T(1024)S(1)}, s32[8192]{0:T(1024)}, u32[]{:S(2)}) copy-start(s32[8192]{0:T(1024)} %param.17) | copy-start | bytes 98308
  35.1 28.7 %copy-start.1 = (bf16[256,1,1408]{2,0,1:T(8,128)(2,1)S(1)}, bf16[256,1,1408]{2,0,1:T(8,128)(2,1)}, u32[]{:S(2)}) copy-start(bf16[256,1,1408]{2,0,1:T(8,128)(2,1)} %param.18) | copy-start | bytes 2162692
  35.1 3.2 %collective-permute-start.2 = (f32[128,1408]{1,0:T(8,128)S(1)}, f32[128,1408]{1,0:T(8,128)}, u32[]{:S(2)}, u32[]{:S(2)}) collective-permute-start(f32[128,1408]{1,0:T(8,128)S(1)} %fusion.78), channel_id=1, source_target_pairs={{0,64},{64,0},{1,65},{65,1},{2,66},{66,2},{3,67},{67,3},{4,68},{68... | collective-permute-start | bytes 2162696 | tf_op jit(solution)/shard_map/ppermute | solution.py:154
  41.6 22.1 %all-to-all-start = ((bf16[64,2,1408]{2,1,0:T(2,128)(2,1)}), bf16[64,2,1408]{2,1,0:T(2,128)(2,1)S(1)}, u32[]{:S(2)}, u32[]{:S(2)}) async-start(bf16[64,2,1408]{2,1,0:T(2,128)(2,1)} %fusion.57), calls=%async_computation | async-start | bytes 720896 | tf_op jit(solution)/shard_map/all_to_all | solution.py:240
  52.8 82.7 %all-gather.3.cloned.1.call-start = ((), (), s32[]{:S(2)}) async-start(), calls=%async_computation.1 | async-start | bytes 5857280 | tf_op jit(solution)/shard_map/all_gather | solution.py:271
  65.4 4.3 %copy-start.3 = (s32[256,64]{0,1:T(8,128)S(1)}, s32[256,64]{0,1:T(8,128)}, u32[]{:S(2)}) copy-start(s32[256,64]{0,1:T(8,128)} %param.19) | copy-start | bytes 196612
  67.9 5.7 %collective-permute-start.3 = (bf16[704,1408]{1,0:T(8,128)(2,1)}, bf16[704,1408]{1,0:T(8,128)(2,1)}, u32[]{:S(2)}, u32[]{:S(2)}) collective-permute-start(bf16[704,1408]{1,0:T(8,128)(2,1)} %param.25), channel_id=1, source_target_pairs={{0,64},{64,0},{1,65},{65,1},{2,66},{66,2},{3,67},{67,3},{4,68},{68... | collective-permute-start | bytes 5947400 | tf_op jit(solution)/shard_map/ppermute | solution.py:154
  175.5 3.0 %collective-permute-start.4 = (bf16[8,256,88]{2,1,0:T(8,128)(2,1)}, bf16[8,256,88]{2,1,0:T(8,128)(2,1)S(1)}, u32[]{:S(2)}, u32[]{:S(2)}) collective-permute-start(bf16[8,256,88]{2,1,0:T(8,128)(2,1)} %shard_map.136), channel_id=1, source_target_pairs={{0,64},{64,0},{1,65},{65,1},{2,66},{66,2},{3,67},{67,3},{4,68},{68... | collective-permute-start | bytes 1081352 | tf_op jit(solution)/shard_map/ppermute | solution.py:154
Sparse Core Ops, SparseCore 0:
  68.0 67.4 all-gather.2

commit v3 on v0

--- a/solution.py
+++ b/solution.py
@@ -237,6 +237,14 @@
     per_peer = merged_count // seq_count
     run_starts = dest_positions.reshape(seq_count, merged_count)[:, 0]
     own_start = run_starts[seq_index]
+    def key_value(rows_in):
+        normed_rows = root_norm(rows_in).astype(jnp.bfloat16)
+        paired = jnp.dot(
+            normed_rows, decoder_kv.reshape(D, -1), preferred_element_type=jnp.float32
+        ).reshape(rows_in.shape[0], 2, HEAD)
+        return (root_norm(paired[:, 0]).astype(jnp.bfloat16), paired[:, 1].astype(jnp.bfloat16))
+
+    text_kv = key_value(text_embeds.reshape(text_embeds.shape[0], D))
     received = lax.all_to_all(
         jnp.transpose(
             jnp.roll(image_rows.reshape(per_peer, seq_count, D), own_start, axis=1), (1, 0, 2)
@@ -261,11 +269,9 @@
             preferred_element_type=jnp.float32,
         )
     ).astype(jnp.bfloat16)
-    paired = jnp.dot(
-        text_normed, decoder_kv.reshape(D, -1), preferred_element_type=jnp.float32
-    ).reshape(text_rows, 2, HEAD)
-    key_rows = root_norm(paired[:, 0]).astype(jnp.bfloat16)
-    value_rows = paired[:, 1].astype(jnp.bfloat16)
+    received_kv = key_value(received.reshape(-1, D))
+    key_rows = text_kv[0].at[landing.T.reshape(-1)].set(received_kv[0])
+    value_rows = text_kv[1].at[landing.T.reshape(-1)].set(received_kv[1])
 
     shared = jnp.stack([key_rows, value_rows], 0)[None]
     piece = lax.all_gather(shared, "seq", axis=0, tiled=True)

time: 192 us -> 204 us (1.062)
  local copies, waits for them, and re-layouts: 16.7 us -> 25.1 us
  matrix products: 28.2 us -> 31.8 us
  other arithmetic: 18.7 us -> 21.3 us
    convert_element_type x1 -> x7, local copies, waits for them, and re-layouts: 0.01 us -> 2.23 us  [the longest x4 1.13 us: key_value(): paired[:, 1].astype(jnp.bfloat16)]
    all_gather x1, waiting for transfers between devices: 49.5 us -> 47.3 us  [body(): piece = lax.all_gather(shared, 'seq', axis=0, tiled=True)]
    scatter x0 -> x2, local copies, waits for them, and re-layouts: none -> 2.15 us  [the longest x1 1.08 us: body(): key_rows = text_kv[0].at[landing.T.reshape(-1)].set(received_kv[0])]
  transfers between devices with their start and end apart: 7 -> 7, of which waited for: 4 -> 5; matrix products, arithmetic and copies ran while one was open for 17% -> 20% of each run, Pallas kernels for 0% -> 0%
where the time goes in v3:
time: 204 us
  waiting for transfers between devices  62.7 us (31%)
  matrix products  31.8 us (16%)
  Pallas kernels  30.7 us (15%)
  local copies, waits for them, and re-layouts  25.1 us (12%)
  other arithmetic  21.3 us (10%)
  starting transfers between devices  16.5 us (8%)
  between operations  15.8 us (8%)
    all_gather x1, waiting for transfers between devices, body(): piece = lax.all_gather(shared, 'seq', axis=0, tiled=True)  47.3 us
    pallas_call x1, Pallas kernels, text_attention(): pl.pallas_call(functools.partial(_text_kernel, scale=scale), grid_spec=pl...  30.7 us
    all_to_all x1, starting transfers between devices, body(): lax.all_to_all(jnp.transpose(jnp.roll(image_rows.reshape(per_peer, seq_co...  11.2 us
    all_gather x1, local copies, waits for them, and re-layouts, body(): piece = lax.all_gather(shared, 'seq', axis=0, tiled=True)  9.83 us
    all_to_all x1, waiting for transfers between devices, body(): lax.all_to_all(jnp.transpose(jnp.roll(image_rows.reshape(per_peer, seq_co...  9 us
    ppermute x5, waiting for transfers between devices, swap(): return lax.ppermute(values, 'section', [(0, 1), (1, 0)])  6.29 us
    select_n x1, other arithmetic, in_head_order(): jnp.where(first, jnp.concatenate([own, other], axis), jnp.concatenate([ot...  6.23 us
    dot_general x1, matrix products, body(): jnp.dot(normed, vision_qkv.reshape(D, -1), preferred_element_type=jnp.flo...  5.99 us
  transfers between devices with their start and end apart: 7, of which 5 were waited for; matrix products, arithmetic and copies ran while one was open for 20% of the time, Pallas kernels for 0%

profile of v3, /device:TPU:1, one launch (start us, length us, event | category | flops | bytes accessed | tf_op | source)
XLA Modules:
  0.0 203.9 jit_solution(13361513223800124201)
XLA Ops:
  6.5 1.3 copy.108
  7.8 1.4 collective-permute-start.1
  9.2 0.7 slice_bitcast_fusion.4
  9.9 0.8 fusion.76
  11.3 1.7 convert_reduce_fusion
  13.0 1.9 fusion.13
  14.9 6.0 %fusion.29 = f32[512,3,8,88]{0,3,2,1:T(8,128)S(1)} fusion(bf16[3,8,88,1408]{3,2,1,0:T(8,128)(2,1)} %bitcast.149, bf16[512,1408]{1,0:T(8,128)(2,1)S(1)} %copy-done.1, f32[512]{0:T(512)S(1)} %add_rsqrt_fusion.4, f32[512]{0:T(512)S(1)} %broadcast_multiply_fusion), kind=kOutput, calls=%fused_computation.32 | convolution fusion | flops 3047948288 | bytes 11718656 | tf_op jit(solution)/shard_map/dot_general | solution.py:190
  21.6 2.5 %fusion = (f32[8,512]{1,0:T(8,128)S(1)}, f32[8,512,512]{1,2,0:T(8,128)S(1)}) fusion(pred[512,512]{0,1:T(8,128)(4,1)S(1)} %broadcast_compare_fusion, f32[512,3,8,88]{0,3,2,1:T(8,128)S(1)} %fusion.29, f32[512,8]{0,1:T(8,128)S(1)} %get-tuple-element.27, f32[512,8]{0,1:T(8,128)S(1)} %get-tuple-element.28), kind=kOutput, calls=%fused_computation.4 | convolution fusion | flops 376827904 | bytes 11583488 | tf_op jit(solution)/shard_map/qhd,khd->hqk/dot_general | solution.py:200
  24.2 1.8 divide_convert_fusion
  26.0 1.2 convolution_convert_fusion
  27.7 0.5 fusion.41
  28.2 0.7 copy-done.3
  29.0 1.6 convolution_convert_fusion.1
  30.6 0.5 constant_dynamic-slice_fusion
  33.1 2.1 %fusion.60 = f32[256,1408]{1,0:T(8,128)S(1)} fusion(bf16[512,1408]{1,0:T(8,128)(2,1)} %param.14, s32[256]{0:T(256)S(1)} %eq.79), kind=kOutput, calls=%fused_computation.80 | convolution fusion | flops 369229824 | bytes 2884608 | tf_op jit(solution)/shard_map/dot_general | solution.py:227
  35.2 3.9 %fusion.19 = bf16[256,1408]{1,0:T(8,128)(2,1)} fusion(f32[256,1408]{1,0:T(8,128)S(1)} %fusion.60, bf16[704,1408]{1,0:T(8,128)(2,1)} %collective-permute-done.1, bf16[704,1408]{1,0:T(8,128)(2,1)S(1)} %copy-done.8, bf16[256,704]{0,1:T(8,128)(2,1)} %collective-permute-done, bf16[256,704]{0,1:T(8,128)(2,1)S(1)} %convolution_convert_fusion.1), kind=kOutput, calls=%fused_computation.24 | convolution fusion | flops 1025114112 | bytes 6848512 | tf_op jit(solution)/shard_map/dot_general | solution.py:228
  39.2 1.3 reshape.484
  40.5 5.4 %fusion.83 = f32[128,1408]{1,0:T(8,128)} fusion(bf16[128,2816]{1,0:T(8,128)(2,1)S(1)} %reshape.484, bf16[2816,1408]{1,0:T(8,128)(2,1)} %bitcast.140), kind=kOutput, calls=%fused_computation.170 | convolution fusion | flops 1015021568 | bytes 9371648 | tf_op jit(solution)/shard_map/dot_general | solution.py:230
  46.0 0.5 collective-permute-start.2
  46.9 1.8 collective-permute-done.2
  48.6 1.4 add_convert_fusion
  50.4 1.7 fusion.65
  52.1 11.2 %all-to-all-start = ((bf16[64,2,1408]{2,1,0:T(2,128)(2,1)}), bf16[64,2,1408]{2,1,0:T(2,128)(2,1)S(1)}, u32[]{:S(2)}, u32[]{:S(2)}) async-start(bf16[64,2,1408]{2,1,0:T(2,128)(2,1)} %fusion.65), calls=%async_computation | async-start | bytes 720896 | tf_op jit(solution)/shard_map/all_to_all | solution.py:248
  63.3 0.9 fusion.69
  64.4 0.5 fusion.73
  64.9 9.0 %all-to-all-done = bf16[64,2,1408]{2,1,0:T(2,128)(2,1)S(1)} async-done(((bf16[64,2,1408]{2,1,0:T(2,128)(2,1)}), bf16[64,2,1408]{2,1,0:T(2,128)(2,1)S(1)}, u32[]{:S(2)}, u32[]{:S(2)}) %all-to-all-start) | async-done | bytes 360480 | tf_op jit(solution)/shard_map/all_to_all | solution.py:248
  73.9 0.4 fusion.37
  74.7 0.9 reshape.521
  75.6 1.5 fusion.61
  77.4 1.1 scatter_fusion.1
  78.5 1.1 scatter_fusion.2
  79.6 0.7 copy.98
  80.3 2.0 collective-permute-start.3
  82.6 0.6 pad_add_fusion.1.info_ref
  83.1 3.2 %collective-permute-done.3 = bf16[704,1408]{1,0:T(8,128)(2,1)} collective-permute-done((bf16[704,1408]{1,0:T(8,128)(2,1)}, bf16[704,1408]{1,0:T(8,128)(2,1)}, u32[]{:S(2)}, u32[]{:S(2)}) %collective-permute-start.3) | collective-permute-done | bytes 1982496 | tf_op jit(solution)/shard_map/ppermute | solution.py:154
  86.3 6.2 %maximum_select_fusion = bf16[1408,1408]{1,0:T(8,128)(2,1)} fusion(bf16[704,1408]{1,0:T(8,128)(2,1)} %collective-permute-done.3, bf16[704,1408]{1,0:T(8,128)(2,1)} %param.25, pred[]{:T(512)S(6)} %eq.90), kind=kLoop, calls=%fused_computation.14 | loop fusion | flops 17842176 | bytes 7929857 | tf_op jit(solution)/shard_map/jit(_where)/select_n | solution.py:158
  92.7 1.8 scatter_fusion
  94.7 0.8 fusion.45
  95.6 1.3 copy.91
  96.9 1.6 fusion.33
  98.5 2.4 %fusion.34.q_ref = bf16[8,256,88]{2,1,0:T(8,128)(2,1)} fusion(f32[256,8,88]{2,0,1:T(8,128)} %copy.91, f32[8,256]{1,0:T(8,128)S(1)} %add_rsqrt_fusion.3), kind=kLoop, calls=%fused_computation.50 | loop fusion | flops 360448 | bytes 1089536 | tf_op jit(solution)/shard_map/convert_element_type | solution.py:271
  100.9 47.3 %all-gather.3.cloned.1.call-done = bf16[128,256,88]{1,2,0:T(8,128)(2,1)} async-done(((bf16[2,256,88]{1,2,0:T(8,128)(2,1)}), bf16[128,256,88]{1,2,0:T(8,128)(2,1)}) %all-gather.3.cloned.1.call-update) | async-done | bytes 5767184 | tf_op jit(solution)/shard_map/all_gather | solution.py:277
  148.2 9.8 %copy.99 = bf16[128,256,88]{2,1,0:T(8,128)(2,1)} copy(bf16[128,256,88]{1,2,0:T(8,128)(2,1)} %all-gather.3.cloned.1.call-done) | data formatting | bytes 11534336 | tf_op jit(solution)/shard_map/all_gather | solution.py:277
  158.0 30.7 %shard_map.136 = bf16[8,256,88]{2,1,0:T(8,128)(2,1)} custom-call(s32[10]{0:T(128)} %constant.143.clone.query_block_ref, s32[10]{0:T(128)} %constant.144.clone.key_block_ref, s32[8]{0:T(128)} %pad_add_fusion.1.info_ref, bf16[8,256,88]{2,1,0:T(8,128)(2,1)} %fusion.34.q_ref, bf16[64,2,256,88]{3,2,1,0:T(8,128)(2,1)} %bitcast.139), custom_call_target="tpu_custom_call" | custom-call | tf_op jit(solution)/shard_map/pallas_call | solution.py:133
  188.8 1.2 copy.100
  190.0 1.3 collective-permute-start.4
  191.3 1.3 collective-permute-done.4
  192.6 4.4 %fusion.22 = bf16[256,1,1408]{2,0,1:T(8,128)(2,1)} fusion(bf16[1408,1408]{1,0:T(8,128)(2,1)} %maximum_select_fusion, bf16[256,1408]{1,0:T(8,128)(2,1)S(1)} %scatter_fusion, bf16[256,704]{0,1:T(8,128)(2,1)S(1)} %collective-permute-done.4, bf16[256,704]{0,1:T(8,128)(2,1)S(1)} %bitcast.147, pred[]{:T(512)S(6)} %eq.90), kind=kOutput, calls=%fused_computation.25 | convolution fusion | flops 1019346944 | bytes 6127617 | tf_op jit(solution)/shard_map/dot_general | solution.py:292
  (67 shorter events, 4.0 us)
Async XLA Ops:
  6.5 88.2 %copy-start = (bf16[1408,704]{0,1:T(8,128)(2,1)S(1)}, bf16[1408,704]{0,1:T(8,128)(2,1)}, u32[]{:S(2)}) copy-start(bf16[1408,704]{0,1:T(8,128)(2,1)} %param.23) | copy-start | bytes 5947396
  7.8 27.4 %collective-permute-start.1 = (bf16[704,1408]{1,0:T(8,128)(2,1)}, bf16[704,1408]{1,0:T(8,128)(2,1)}, u32[]{:S(2)}, u32[]{:S(2)}) collective-permute-start(bf16[704,1408]{1,0:T(8,128)(2,1)} %param.21), channel_id=1, source_target_pairs={{0,64},{64,0},{1,65},{65,1},{2,66},{66,2},{3,67},{67,3},{4,68},{68... | collective-permute-start | bytes 5947400 | tf_op jit(solution)/shard_map/ppermute | solution.py:154
  11.3 3.6 %copy-start.1 = (bf16[512,1408]{1,0:T(8,128)(2,1)S(1)}, bf16[512,1408]{1,0:T(8,128)(2,1)}, u32[]{:S(2)}) copy-start(bf16[512,1408]{1,0:T(8,128)(2,1)} %param.14) | copy-start | bytes 4325380
  24.1 3.5 %copy-start.2 = (bf16[1408,2,88]{0,2,1:T(8,128)(2,1)S(1)}, bf16[1408,2,88]{0,2,1:T(8,128)(2,1)}, u32[]{:S(2)}) copy-start(bf16[1408,2,88]{0,2,1:T(8,128)(2,1)} %param.24) | copy-start | bytes 1486852
  25.9 1.2 copy-start.9
  25.9 2.9 %copy-start.6 = (s32[8192]{0:T(1024)S(1)}, s32[8192]{0:T(1024)}, u32[]{:S(2)}) copy-start(s32[8192]{0:T(1024)} %param.17) | copy-start | bytes 98308
  27.2 8.0 %collective-permute-start = (bf16[256,704]{0,1:T(8,128)(2,1)}, bf16[256,704]{0,1:T(8,128)(2,1)}, u32[]{:S(2)}, u32[]{:S(2)}) collective-permute-start(bf16[256,704]{0,1:T(8,128)(2,1)} %convolution_convert_fusion), channel_id=1, source_target_pairs={{0,64},{64,0},{1,65},{65,1},{2,66},{66,2},{3,67},{67,3},{4,68},{68... | collective-permute-start | bytes 1081352 | tf_op jit(solution)/shard_map/ppermute | solution.py:154
  28.2 0.7 copy-start.3
  33.1 2.2 %copy-start.8 = (bf16[704,1408]{1,0:T(8,128)(2,1)S(1)}, bf16[704,1408]{1,0:T(8,128)(2,1)}, u32[]{:S(2)}) copy-start(bf16[704,1408]{1,0:T(8,128)(2,1)} %param.21) | copy-start | bytes 5947396
  40.5 6.0 %copy-start.4 = (f32[256,2,88]{0,2,1:T(8,128)S(1)}, f32[256,2,88]{0,2,1:T(8,128)}, u32[]{:S(2)}) copy-start(f32[256,2,88]{0,2,1:T(8,128)} %copy-done.3) | copy-start | bytes 540676
  46.0 2.7 %collective-permute-start.2 = (f32[128,1408]{1,0:T(8,128)}, f32[128,1408]{1,0:T(8,128)}, u32[]{:S(2)}, u32[]{:S(2)}) collective-permute-start(f32[128,1408]{1,0:T(8,128)} %fusion.83), channel_id=1, source_target_pairs={{0,64},{64,0},{1,65},{65,1},{2,66},{66,2},{3,67},{67,3},{4,68},{68... | collective-permute-start | bytes 2162696 | tf_op jit(solution)/shard_map/ppermute | solution.py:154
  52.1 21.8 %all-to-all-start = ((bf16[64,2,1408]{2,1,0:T(2,128)(2,1)}), bf16[64,2,1408]{2,1,0:T(2,128)(2,1)S(1)}, u32[]{:S(2)}, u32[]{:S(2)}) async-start(bf16[64,2,1408]{2,1,0:T(2,128)(2,1)} %fusion.65), calls=%async_computation | async-start | bytes 720896 | tf_op jit(solution)/shard_map/all_to_all | solution.py:248
  63.3 84.9 %all-gather.3.cloned.1.call-start = ((), (), s32[]{:S(2)}) async-start(), calls=%async_computation.1 | async-start | bytes 5857280 | tf_op jit(solution)/shard_map/all_gather | solution.py:277
  75.6 6.8 %copy-start.5 = (s32[256,64]{0,1:T(8,128)S(1)}, s32[256,64]{0,1:T(8,128)}, u32[]{:S(2)}) copy-start(s32[256,64]{0,1:T(8,128)} %param.19) | copy-start | bytes 196612
  80.3 6.0 %collective-permute-start.3 = (bf16[704,1408]{1,0:T(8,128)(2,1)}, bf16[704,1408]{1,0:T(8,128)(2,1)}, u32[]{:S(2)}, u32[]{:S(2)}) collective-permute-start(bf16[704,1408]{1,0:T(8,128)(2,1)} %param.25), channel_id=1, source_target_pairs={{0,64},{64,0},{1,65},{65,1},{2,66},{66,2},{3,67},{67,3},{4,68},{68... | collective-permute-start | bytes 5947400 | tf_op jit(solution)/shard_map/ppermute | solution.py:154
  83.1 9.6 %copy-start.7 = (s32[128]{0:T(128)S(1)}, s32[128]{0:T(128)}, u32[]{:S(2)}) copy-start(s32[128]{0:T(128)} %fusion.73) | copy-start | bytes 1540
  190.0 2.6 %collective-permute-start.4 = (bf16[256,704]{0,1:T(8,128)(2,1)S(1)}, bf16[256,704]{0,1:T(8,128)(2,1)S(1)}, u32[]{:S(2)}, u32[]{:S(2)}) collective-permute-start(bf16[256,704]{0,1:T(8,128)(2,1)S(1)} %bitcast.146), channel_id=1, source_target_pairs={{0,64},{64,0},{1,65},{65,1},{2,66},{66,2},{3,67},{67,3},{4,68},{68... | collective-permute-start | bytes 1081352 | tf_op jit(solution)/shard_map/ppermute | solution.py:154
Sparse Core Ops, SparseCore 0:
  80.5 67.6 all-gather.2
